TPU v7x, 32 devices: a whole 2x2x4 slice. The times are simulated.
32 devices in a mesh: owner: 2 (over x), reader: 16 (over z, y, core).
Axes of the slice: x: 2, y: 2, z: 4, core: 2. Of those that a mesh axis runs over, the one named last changes fastest.
Arguments:
- acts: bfloat16 [256, 4096], P('reader', 'owner'), may hold values from -6 to 6
- grads: bfloat16 [256, 14336], P('reader', 'owner'), may hold values from -6 to 6
- basis_a: bfloat16 [4096, 4096], P('reader', 'owner'), may hold values from -0.09375 to 0.09375
- basis_g: bfloat16 [14336, 14336], P('reader', 'owner'), may hold values from -0.046875 to 0.046875
- eigvals: bfloat16 [14336, 4096], P('reader', 'owner'), may hold values from 0.099609375 to 10
- lengths: int32 [2], replicated, may hold values from 1 to 128, as said below
- shuffle: int32 [2], replicated, may hold values from 0 to 1, each once
Outputs:
- token_score: float32 [256], P('owner')
- example_score: float32 [2], replicated
Inputs may be any that keep to these rules, and one draw needn't show every extreme that they name: `lengths`: some slot has exactly 128 live tokens. `shuffle`: each example id appears once.
All inputs are finite; a program needn't handle non-finite values.
Results may differ from a plain program's by a relative error of at most 0.0003.
Values may be sent and summed in bfloat16 or wider, within the bound.
No kernel may reach another device: no remote copies, remote signals or barrier semaphores. Data moves between devices by JAX's collectives and lax.ppermute only.
A program may use at most 128 MiB of HBM per device.

v0:
```python
import jax
import jax.numpy as jnp
from jax import lax
from jax.sharding import PartitionSpec as P

D = 4096
FF = 14336
SEQ = 128


def local(acts, grads, basis_a, basis_g, eigvals, lengths, shuffle):
    owner_index = lax.axis_index("owner")
    own_length = lax.dynamic_index_in_dim(lengths, owner_index, 0, keepdims=False)
    positions = jnp.arange(SEQ, dtype=jnp.int32)
    live = (positions < own_length).astype(jnp.float32)
    partial_g = jnp.einsum(
        "tk,jk->tj",
        lax.all_gather(grads, "reader", axis=0, tiled=True),
        basis_g,
        preferred_element_type=jnp.float32,
    )
    own_g = lax.psum_scatter(partial_g, "owner", scatter_dimension=0, tiled=True)
    rot_g = (own_g * live[:, None]).astype(jnp.bfloat16)
    all_rows = lax.all_gather(acts, "reader", axis=0, tiled=True)
    own_rows = lax.all_to_all(all_rows, "owner", split_axis=0, concat_axis=1, tiled=True)
    vectors = lax.all_gather(basis_a, "owner", axis=1, tiled=True)
    own_a = jnp.einsum("tk,jk->tj", own_rows, vectors, preferred_element_type=jnp.float32)
    rot_a = (own_a * live[:, None]).astype(jnp.bfloat16)
    full_a = lax.all_gather(rot_a, "reader", axis=1, tiled=True)
    eigen_block = lax.all_gather(eigvals, "owner", axis=1, tiled=True)
    outer = jnp.einsum("tm,tn->mn", rot_g, full_a, preferred_element_type=jnp.float32)
    scaled = (outer / eigen_block.astype(jnp.float32)).astype(jnp.bfloat16)
    projected = jnp.dot(rot_g, scaled, preferred_element_type=jnp.float32)
    partial_score = jnp.sum(projected * full_a.astype(jnp.float32), axis=1) / (FF * D)
    token_score = lax.psum(partial_score, "reader")
    slot_mean = jnp.sum(token_score, keepdims=True) / SEQ
    all_means = lax.all_gather(slot_mean, "owner", axis=0, tiled=True)
    count = shuffle.shape[0]
    table = (shuffle[:, None] == jnp.arange(count, dtype=jnp.int32)[None, :]).astype(jnp.float32)
    example_score = jnp.sum(all_means[:, None] * table, axis=0)
    return (token_score, example_score)


def solution(mesh):
    return jax.shard_map(
        local,
        mesh=mesh,
        in_specs=(
            P("reader", "owner"),
            P("reader", "owner"),
            P("reader", "owner"),
            P("reader", "owner"),
            P("reader", "owner"),
            P(),
            P(),
        ),
        out_specs=(P("owner"), P()),
        check_vma=False,
    )
```

profile of v0, /device:TPU:0, one launch (start us, length us, event | category | flops | bytes accessed | tf_op | source)
XLA Modules:
  0.0 346.0 jit_solution(8944493307228276584)
XLA Ops:
  7.2 0.0 all-gather.8.cloned.1.call-start
  7.2 0.7 all-gather.8.cloned.1.call-update
  7.9 0.0 all-gather.10.cloned.1.call-start
  7.9 0.7 all-gather.10.cloned.1.call-update
  8.6 0.0 all-gather.6.cloned.1.call-start
  8.7 0.7 all-gather.6.cloned.1.call-update
  9.4 41.5 %all-gather.8.cloned.1.call-done = bf16[256,2048]{1,0:T(8,128)(2,1)} async-done(((bf16[16,2048]{1,0:T(8,128)(2,1)}), bf16[256,2048]{1,0:T(8,128)(2,1)}) %all-gather.8.cloned.1.call-update) | async-done | bytes 1048592 | tf_op jit(solution)/shard_map/all_gather | solution.py:24
  50.8 3.6 %all-to-all-start = ((bf16[2,128,2048]{2,1,0:T(8,128)(2,1)}), bf16[2,128,2048]{2,1,0:T(8,128)(2,1)S(1)}, u32[]{:S(2)}, u32[]{:S(2)}) async-start(bf16[2,128,2048]{2,1,0:T(8,128)(2,1)} %bitcast.13), calls=%async_computation.1 | async-start | bytes 2097152 | tf_op jit(solution)/shard_map/all_to_all | solution.py:25
  54.4 0.0 all-gather.12.cloned.1.call-start
  54.5 1.2 dynamic_slice.4
  55.7 0.6 compare_convert_fusion
  56.4 19.8 %all-to-all-done = bf16[2,128,2048]{2,1,0:T(8,128)(2,1)S(1)} async-done(((bf16[2,128,2048]{2,1,0:T(8,128)(2,1)}), bf16[2,128,2048]{2,1,0:T(8,128)(2,1)S(1)}, u32[]{:S(2)}, u32[]{:S(2)}) %all-to-all-start) | async-done | bytes 1048608 | tf_op jit(solution)/shard_map/all_to_all | solution.py:25
  76.2 0.7 copy.10
  76.9 14.5 %all-gather.10.cloned.1.call-done = bf16[256,4096]{1,0:T(8,128)(2,1)} async-done(((bf16[256,2048]{1,0:T(8,128)(2,1)}), bf16[256,4096]{1,0:T(8,128)(2,1)}) %all-gather.10.cloned.1.call-update) | async-done | bytes 2097168 | tf_op jit(solution)/shard_map/all_gather | solution.py:26
  91.4 3.1 fusion.5
  94.5 0.0 all-gather.12.cloned.1.call-update
  94.5 0.0 all-gather.14.cloned.1.call-start
  94.6 0.5 all-gather.14.cloned.1.call-update
  95.1 0.0 copy-start.1
  95.1 0.0 reduce-scatter.2.cloned.1.call-start
  95.2 44.1 %all-gather.6.cloned.1.call-done = bf16[256,7168]{1,0:T(8,128)(2,1)} async-done(((bf16[16,7168]{1,0:T(8,128)(2,1)}), bf16[256,7168]{1,0:T(8,128)(2,1)}) %all-gather.6.cloned.1.call-update) | async-done | bytes 3670032 | tf_op jit(solution)/shard_map/all_gather | solution.py:18
  139.3 10.7 %fusion.9 = f32[256,896]{1,0:T(8,128)} fusion(bf16[256,7168]{1,0:T(8,128)(2,1)} %all-gather.6.cloned.1.call-done, bf16[896,7168]{1,0:T(8,128)(2,1)} %param.10), kind=kOutput, calls=%fused_computation.13 | convolution fusion | flops 3288334336 | bytes 17432576 | tf_op jit(solution)/shard_map/tk,jk->tj/dot_general | solution.py:16
  149.9 0.0 reduce-scatter.2.cloned.1.call-update
  150.0 0.0 copy-done.1
  150.0 0.6 dynamic-slice
  150.5 0.0 copy-start
  150.5 26.6 %all-gather.12.cloned.1.call-done = bf16[128,4096]{1,0:T(8,128)(2,1)} async-done(((bf16[128,256]{1,0:T(8,128)(2,1)}), bf16[128,4096]{1,0:T(8,128)(2,1)}) %all-gather.12.cloned.1.call-update) | async-done | bytes 1048592 | tf_op jit(solution)/shard_map/all_gather | solution.py:29
  177.1 93.1 %all-gather.14.cloned.1.call-done = bf16[896,4096]{1,0:T(8,128)(2,1)} async-done(((bf16[896,2048]{1,0:T(8,128)(2,1)}), bf16[896,4096]{1,0:T(8,128)(2,1)}) %all-gather.14.cloned.1.call-update) | async-done | bytes 7340048 | tf_op jit(solution)/shard_map/all_gather | solution.py:30
  270.3 21.0 %reduce-scatter.2.cloned.1.call-done = f32[128,896]{1,0:T(8,128)} async-done(((f32[256,896]{1,0:T(8,128)}), f32[128,896]{1,0:T(8,128)}) %reduce-scatter.2.cloned.1.call-update) | async-done | bytes 458768 | tf_op jit(solution)/shard_map/reduce_scatter | solution.py:22
  291.3 7.3 %fusion.4 = f32[128]{0:T(128)S(1)} fusion(bf16[128,4096]{1,0:T(8,128)(2,1)} %all-gather.12.cloned.1.call-done, bf16[896,4096]{1,0:T(8,128)(2,1)} %all-gather.14.cloned.1.call-done, f32[128,896]{1,0:T(8,128)} %reduce-scatter.2.cloned.1.call-done, f32[128]{0:T(128)S(1)} %compare_convert_fusion), kind=kOutput, calls=%fused_computation.4 | convolution fusion | flops 1892089728 | bytes 8848384 | tf_op jit(solution)/shard_map/dot_general | solution.py:33
  298.6 33.2 %psum.7 = f32[128]{0:T(128)S(1)} all-reduce(f32[128]{0:T(128)S(1)} %broadcast_multiply_fusion), channel_id=1, replica_groups=mesh['owner'=2,'reader'=16] {'reader'}, use_global_device_ids=true, to_apply=%region_2.3 | all-reduce | flops 128 | bytes 1024 | tf_op jit(solution)/shard_map/psum | solution.py:35
  331.7 0.0 copy-start.2
  331.7 0.6 reduce_sum.28
  333.0 0.7 dynamic-update-slice
  333.7 4.9 %all-reduce = f32[2]{0:T(128)S(1)} all-reduce(f32[2]{0:T(128)S(1)} %dynamic-update-slice), channel_id=1, replica_groups=mesh['owner'=2,'reader'=16] {'owner'}, use_global_device_ids=true, to_apply=%add | all-reduce | flops 2 | bytes 16
  338.6 0.0 copy-done
  338.6 0.6 fusion.8
  339.2 0.0 copy-done.2
  (2 shorter events, 0.0 us)
Async XLA Ops:
  7.2 43.7 %all-gather.8.cloned.1.call-start = ((), (), s32[]{:S(2)}) async-start(), calls=%async_computation.4 | async-start | bytes 1114112 | tf_op jit(solution)/shard_map/all_gather | solution.py:24
  7.9 83.5 %all-gather.10.cloned.1.call-start = ((), (), s32[]{:S(2)}) async-start(), calls=%async_computation.5 | async-start | bytes 3145728 | tf_op jit(solution)/shard_map/all_gather | solution.py:26
  8.6 130.6 %all-gather.6.cloned.1.call-start = ((), (), s32[]{:S(2)}) async-start(), calls=%async_computation.2 | async-start | bytes 3899392 | tf_op jit(solution)/shard_map/all_gather | solution.py:18
  50.8 25.4 %all-to-all-start = ((bf16[2,128,2048]{2,1,0:T(8,128)(2,1)}), bf16[2,128,2048]{2,1,0:T(8,128)(2,1)S(1)}, u32[]{:S(2)}, u32[]{:S(2)}) async-start(bf16[2,128,2048]{2,1,0:T(8,128)(2,1)} %bitcast.13), calls=%async_computation.1 | async-start | bytes 2097152 | tf_op jit(solution)/shard_map/all_to_all | solution.py:25
  54.4 122.7 %all-gather.12.cloned.1.call-start = ((), (), s32[]{:S(2)}) async-start(), calls=%async_computation.6 | async-start | bytes 1114112 | tf_op jit(solution)/shard_map/all_gather | solution.py:29
  94.5 175.7 %all-gather.14.cloned.1.call-start = ((), (), s32[]{:S(2)}) async-start(), calls=%async_computation.7 | async-start | bytes 11010048 | tf_op jit(solution)/shard_map/all_gather | solution.py:30
  95.1 54.9 %copy-start.1 = (u32[32]{0:T(128)S(1)}, u32[32]{0:T(128)}, u32[]{:S(2)}) copy-start(u32[32]{0:T(128)} %constant.24) | copy-start | bytes 388
  95.1 196.1 %reduce-scatter.2.cloned.1.call-start = ((), (), s32[]{:S(2)}) async-start(), calls=%async_computation.3 | async-start | bytes 1376256 | tf_op jit(solution)/shard_map/reduce_scatter | solution.py:22
  150.5 188.0 %copy-start = (s32[2]{0:T(128)S(1)}, s32[2]{0:T(128)}, u32[]{:S(2)}) copy-start(s32[2]{0:T(128)} %param.13) | copy-start | bytes 28
  331.7 7.4 %copy-start.2 = (f32[128]{0:T(128)}, f32[128]{0:T(128)S(1)}, u32[]{:S(2)}) copy-start(f32[128]{0:T(128)S(1)} %psum.7) | copy-start | bytes 1540
Sparse Core Ops, SparseCore 0:
  10.2 40.6 all-gather.7
  52.4 39.0 all-gather.9
  93.7 45.4 all-gather.5
  141.3 35.8 all-gather.11
  178.5 91.6 all-gather.13
  272.4 18.8 reduce-scatter.1
where the time goes:
time: 346 us
  waiting for transfers between devices  263 us (76%)
  blocking collectives  38.1 us (11%)
  matrix products  21.1 us (6%)
  between operations  14.8 us (4%)
  starting transfers between devices  3.81 us (1%)
    all_gather x1, waiting for transfers between devices, local(): eigen_block = lax.all_gather(eigvals, 'owner', axis=1, tiled=True)  93.1 us
    all_gather x1, waiting for transfers between devices, local(): lax.all_gather(grads, 'reader', axis=0, tiled=True)  44.1 us
    all_gather x1, waiting for transfers between devices, local(): all_rows = lax.all_gather(acts, 'reader', axis=0, tiled=True)  41.5 us
    psum x1, blocking collectives, local(): token_score = lax.psum(partial_score, 'reader')  33.2 us
    all_gather x1, waiting for transfers between devices, local(): full_a = lax.all_gather(rot_a, 'reader', axis=1, tiled=True)  26.6 us
    reduce_scatter x1, waiting for transfers between devices, local(): lax.psum_scatter(partial_g, 'owner', scatter_dimension=0, tiled=True)  21 us
    all_to_all x1, waiting for transfers between devices, local(): lax.all_to_all(all_rows, 'owner', split_axis=0, concat_axis=1, tiled=True)  19.8 us
    all_gather x1, waiting for transfers between devices, local(): vectors = lax.all_gather(basis_a, 'owner', axis=1, tiled=True)  14.5 us
  transfers between devices with their start and end apart: 7, of which 7 were waited for; matrix products, arithmetic and copies ran while one was open for 5% of the time, Pallas kernels for 0%

commit v1 on v0

--- a/solution.py
+++ b/solution.py
@@ -21,7 +21,15 @@
     )
     own_g = lax.psum_scatter(partial_g, "owner", scatter_dimension=0, tiled=True)
     rot_g = (own_g * live[:, None]).astype(jnp.bfloat16)
-    all_rows = lax.all_gather(acts, "reader", axis=0, tiled=True)
+    ways, here = (lax.axis_size("reader"), lax.axis_index("reader"))
+    grown, reach = (acts, 1)
+    while reach < ways:
+        theirs = lax.ppermute(grown, "reader", [(d, d ^ reach) for d in range(ways)])
+        mine_first = jnp.concatenate([grown, theirs], axis=0)
+        theirs_first = jnp.concatenate([theirs, grown], axis=0)
+        grown = jnp.where(here & reach == 0, mine_first, theirs_first)
+        reach = 2 * reach
+    all_rows = grown
     own_rows = lax.all_to_all(all_rows, "owner", split_axis=0, concat_axis=1, tiled=True)
     vectors = lax.all_gather(basis_a, "owner", axis=1, tiled=True)
     own_a = jnp.einsum("tk,jk->tj", own_rows, vectors, preferred_element_type=jnp.float32)

time: 346 us -> 302 us (0.87)
  waiting for transfers between devices: 263 us -> 210 us
  starting transfers between devices: 3.81 us -> 11.7 us
    all_gather x1 -> x0, waiting for transfers between devices: 41.5 us -> none  [local(): all_rows = lax.all_gather(acts, 'reader', axis=0, tiled=True)]
    ppermute x0 -> x4, waiting for transfers between devices: none -> 33.3 us  [local(): lax.ppermute(grown, 'reader', [(d, d ^ reach) for d in range(ways)])]
    all_gather x1, waiting for transfers between devices: 44.1 us -> 21.6 us  [local(): lax.all_gather(grads, 'reader', axis=0, tiled=True)]
    all_gather x1, waiting for transfers between devices: 14.5 us -> 0.02 us  [local(): vectors = lax.all_gather(basis_a, 'owner', axis=1, tiled=True)]
    ppermute x0 -> x4, starting transfers between devices: none -> 7.87 us  [local(): lax.ppermute(grown, 'reader', [(d, d ^ reach) for d in range(ways)])]
    all_to_all x1, waiting for transfers between devices: 19.8 us -> 12.1 us  [local(): lax.all_to_all(all_rows, 'owner', split_axis=0, concat_axis=1, tiled=True)]
  transfers between devices with their start and end apart: 7 -> 10, of which waited for: 7 -> 9; matrix products, arithmetic and copies ran while one was open for 5% -> 6% of each run, Pallas kernels for 0% -> 0%
where the time goes in v1:
time: 302 us
  waiting for transfers between devices  210 us (70%)
  blocking collectives  38.1 us (13%)
  matrix products  21.1 us (7%)
  between operations  14.5 us (5%)
  starting transfers between devices  11.7 us (4%)
  other arithmetic  4.19 us (1%)
    all_gather x1, waiting for transfers between devices, local(): eigen_block = lax.all_gather(eigvals, 'owner', axis=1, tiled=True)  93.1 us
    ppermute x4, waiting for transfers between devices, local(): lax.ppermute(grown, 'reader', [(d, d ^ reach) for d in range(ways)])  33.3 us
    psum x1, blocking collectives, local(): token_score = lax.psum(partial_score, 'reader')  33.2 us
    all_gather x1, waiting for transfers between devices, local(): full_a = lax.all_gather(rot_a, 'reader', axis=1, tiled=True)  26.6 us
    all_gather x1, waiting for transfers between devices, local(): lax.all_gather(grads, 'reader', axis=0, tiled=True)  21.6 us
    reduce_scatter x1, waiting for transfers between devices, local(): lax.psum_scatter(partial_g, 'owner', scatter_dimension=0, tiled=True)  21 us
    all_to_all x1, waiting for transfers between devices, local(): lax.all_to_all(all_rows, 'owner', split_axis=0, concat_axis=1, tiled=True)  12.1 us
    dot_general x1, matrix products, local(): jnp.einsum('tk,jk->tj', lax.all_gather(grads, 'reader', axis=0, tiled=Tru...  10.7 us
  transfers between devices with their start and end apart: 10, of which 9 were waited for; matrix products, arithmetic and copies ran while one was open for 6% of the time, Pallas kernels for 0%

profile of v1, /device:TPU:0, one launch (start us, length us, event | category | flops | bytes accessed | tf_op | source)
XLA Modules:
  0.0 301.9 jit_solution(6250588924869049884)
XLA Ops:
  7.2 0.0 copy-start
  7.2 0.0 all-gather.7.cloned.1.call-start
  7.2 0.7 all-gather.7.cloned.1.call-update
  7.9 0.0 all-gather.5.cloned.1.call-start
  8.0 0.7 all-gather.5.cloned.1.call-update
  8.7 0.5 collective-permute-start
  9.2 1.1 collective-permute-done
  10.3 0.9 maximum_select_fusion.3
  11.2 2.9 collective-permute-start.1
  14.2 3.8 %collective-permute-done.1 = bf16[32,2048]{1,0:T(8,128)(2,1)S(1)} collective-permute-done((bf16[32,2048]{1,0:T(8,128)(2,1)S(1)}, bf16[32,2048]{1,0:T(8,128)(2,1)S(1)}, u32[]{:S(2)}, u32[]{:S(2)}) %collective-permute-start.1) | collective-permute-done | bytes 131104 | tf_op jit(solution)/shard_map/ppermute | solution.py:27
  18.0 1.9 collective-permute-start.2
  19.9 6.1 %collective-permute-done.2 = bf16[64,2048]{1,0:T(8,128)(2,1)S(1)} collective-permute-done((bf16[64,2048]{1,0:T(8,128)(2,1)S(1)}, bf16[64,2048]{1,0:T(8,128)(2,1)S(1)}, u32[]{:S(2)}, u32[]{:S(2)}) %collective-permute-start.2) | collective-permute-done | bytes 262176 | tf_op jit(solution)/shard_map/ppermute | solution.py:27
  26.0 0.1 maximum_select_fusion.1
  26.1 2.6 collective-permute-start.3
  28.6 22.3 %collective-permute-done.3 = bf16[128,2048]{1,0:T(8,128)(2,1)S(1)} collective-permute-done((bf16[128,2048]{1,0:T(8,128)(2,1)S(1)}, bf16[128,2048]{1,0:T(8,128)(2,1)S(1)}, u32[]{:S(2)}, u32[]{:S(2)}) %collective-permute-start.3) | collective-permute-done | bytes 524320 | tf_op jit(solution)/shard_map/ppermute | solution.py:27
  50.9 1.3 maximum_select_fusion
  52.2 3.6 %all-to-all-start = ((bf16[2,128,2048]{2,1,0:T(8,128)(2,1)}), bf16[2,128,2048]{2,1,0:T(8,128)(2,1)S(1)}, u32[]{:S(2)}, u32[]{:S(2)}) async-start(bf16[2,128,2048]{2,1,0:T(8,128)(2,1)} %bitcast.1), calls=%async_computation.1 | async-start | bytes 2097152 | tf_op jit(solution)/shard_map/all_to_all | solution.py:33
  55.8 0.0 all-gather.9.cloned.1.call-start
  55.9 0.0 copy-done
  55.9 0.6 dynamic_slice.4
  56.5 0.6 compare_convert_fusion
  57.1 12.1 %all-to-all-done = bf16[2,128,2048]{2,1,0:T(8,128)(2,1)S(1)} async-done(((bf16[2,128,2048]{2,1,0:T(8,128)(2,1)}), bf16[2,128,2048]{2,1,0:T(8,128)(2,1)S(1)}, u32[]{:S(2)}, u32[]{:S(2)}) %all-to-all-start) | async-done | bytes 1048608 | tf_op jit(solution)/shard_map/all_to_all | solution.py:33
  69.2 0.7 copy.10
  69.9 0.0 all-gather.7.cloned.1.call-done
  69.9 3.1 %fusion.5 = bf16[128,256]{1,0:T(8,128)(2,1)} fusion(bf16[128,4096]{0,1:T(8,128)(2,1)S(1)} %bitcast.12, bf16[256,4096]{1,0:T(8,128)(2,1)} %all-gather.7.cloned.1.call-done, f32[128]{0:T(128)S(1)} %compare_convert_fusion), kind=kOutput, calls=%fused_computation.6 | convolution fusion | flops 268500992 | bytes 3211776 | tf_op jit(solution)/shard_map/tk,jk->tj/dot_general | solution.py:35
  73.0 0.0 all-gather.9.cloned.1.call-update
  73.0 0.0 all-gather.11.cloned.1.call-start
  73.0 0.5 all-gather.11.cloned.1.call-update
  73.6 0.0 copy-start.2
  73.6 0.0 reduce-scatter.2.cloned.1.call-start
  73.6 21.6 %all-gather.5.cloned.1.call-done = bf16[256,7168]{1,0:T(8,128)(2,1)} async-done(((bf16[16,7168]{1,0:T(8,128)(2,1)}), bf16[256,7168]{1,0:T(8,128)(2,1)}) %all-gather.5.cloned.1.call-update) | async-done | bytes 3670032 | tf_op jit(solution)/shard_map/all_gather | solution.py:18
  95.2 10.7 %fusion.9 = f32[256,896]{1,0:T(8,128)} fusion(bf16[256,7168]{1,0:T(8,128)(2,1)} %all-gather.5.cloned.1.call-done, bf16[896,7168]{1,0:T(8,128)(2,1)} %param.10), kind=kOutput, calls=%fused_computation.17 | convolution fusion | flops 3288334336 | bytes 17432576 | tf_op jit(solution)/shard_map/tk,jk->tj/dot_general | solution.py:16
  105.9 0.0 reduce-scatter.2.cloned.1.call-update
  106.0 0.0 copy-done.2
  106.0 0.7 dynamic-slice
  106.6 0.0 copy-start.1
  106.6 26.6 %all-gather.9.cloned.1.call-done = bf16[128,4096]{1,0:T(8,128)(2,1)} async-done(((bf16[128,256]{1,0:T(8,128)(2,1)}), bf16[128,4096]{1,0:T(8,128)(2,1)}) %all-gather.9.cloned.1.call-update) | async-done | bytes 1048592 | tf_op jit(solution)/shard_map/all_gather | solution.py:37
  133.3 93.1 %all-gather.11.cloned.1.call-done = bf16[896,4096]{1,0:T(8,128)(2,1)} async-done(((bf16[896,2048]{1,0:T(8,128)(2,1)}), bf16[896,4096]{1,0:T(8,128)(2,1)}) %all-gather.11.cloned.1.call-update) | async-done | bytes 7340048 | tf_op jit(solution)/shard_map/all_gather | solution.py:38
  226.4 21.0 %reduce-scatter.2.cloned.1.call-done = f32[128,896]{1,0:T(8,128)} async-done(((f32[256,896]{1,0:T(8,128)}), f32[128,896]{1,0:T(8,128)}) %reduce-scatter.2.cloned.1.call-update) | async-done | bytes 458768 | tf_op jit(solution)/shard_map/reduce_scatter | solution.py:22
  247.4 7.3 %fusion.4 = f32[128]{0:T(128)S(1)} fusion(bf16[128,4096]{1,0:T(8,128)(2,1)} %all-gather.9.cloned.1.call-done, bf16[896,4096]{1,0:T(8,128)(2,1)} %all-gather.11.cloned.1.call-done, f32[128,896]{1,0:T(8,128)} %reduce-scatter.2.cloned.1.call-done, f32[128]{0:T(128)S(1)} %compare_convert_fusion), kind=kOutput, calls=%fused_computation.4 | convolution fusion | flops 1892089728 | bytes 8848384 | tf_op jit(solution)/shard_map/dot_general | solution.py:41
  254.7 33.2 %psum.7 = f32[128]{0:T(128)S(1)} all-reduce(f32[128]{0:T(128)S(1)} %broadcast_multiply_fusion), channel_id=1, replica_groups=mesh['owner'=2,'reader'=16] {'reader'}, use_global_device_ids=true, to_apply=%region_2.3 | all-reduce | flops 128 | bytes 1024 | tf_op jit(solution)/shard_map/psum | solution.py:43
  287.8 0.0 copy-start.3
  287.8 0.6 reduce_sum.28
  289.1 0.8 dynamic-update-slice
  289.9 4.9 %all-reduce = f32[2]{0:T(128)S(1)} all-reduce(f32[2]{0:T(128)S(1)} %dynamic-update-slice), channel_id=1, replica_groups=mesh['owner'=2,'reader'=16] {'owner'}, use_global_device_ids=true, to_apply=%add | all-reduce | flops 2 | bytes 16
  294.8 0.0 copy-done.1
  294.8 0.6 fusion.8
  295.4 0.0 copy-done.3
  (3 shorter events, 0.1 us)
Async XLA Ops:
  7.2 48.7 %copy-start = (s32[2]{0:T(128)S(1)}, s32[2]{0:T(128)}, u32[]{:S(2)}) copy-start(s32[2]{0:T(128)} %param.12) | copy-start | bytes 28
  7.2 62.7 %all-gather.7.cloned.1.call-start = ((), (), s32[]{:S(2)}) async-start(), calls=%async_computation.4 | async-start | bytes 3145728 | tf_op jit(solution)/shard_map/all_gather | solution.py:34
  7.9 87.3 %all-gather.5.cloned.1.call-start = ((), (), s32[]{:S(2)}) async-start(), calls=%async_computation.2 | async-start | bytes 3899392 | tf_op jit(solution)/shard_map/all_gather | solution.py:18
  8.7 1.6 collective-permute-start
  11.2 6.8 %collective-permute-start.1 = (bf16[32,2048]{1,0:T(8,128)(2,1)S(1)}, bf16[32,2048]{1,0:T(8,128)(2,1)S(1)}, u32[]{:S(2)}, u32[]{:S(2)}) collective-permute-start(bf16[32,2048]{1,0:T(8,128)(2,1)S(1)} %maximum_select_fusion.3), channel_id=1, source_target_pairs={{0,2},{1,3},{2,0},{3,1},{4,6},{5,7},{6,4},{7,5},{8,10},{9,11},{10,... | collective-permute-start | bytes 393224 | tf_op jit(solution)/shard_map/ppermute | solution.py:27
  18.0 7.9 %collective-permute-start.2 = (bf16[64,2048]{1,0:T(8,128)(2,1)S(1)}, bf16[64,2048]{1,0:T(8,128)(2,1)S(1)}, u32[]{:S(2)}, u32[]{:S(2)}) collective-permute-start(bf16[64,2048]{1,0:T(8,128)(2,1)S(1)} %maximum_select_fusion.2), channel_id=1, source_target_pairs={{0,4},{1,5},{2,6},{3,7},{4,0},{5,1},{6,2},{7,3},{8,12},{9,13},{10,... | collective-permute-start | bytes 786440 | tf_op jit(solution)/shard_map/ppermute | solution.py:27
  26.1 24.9 %collective-permute-start.3 = (bf16[128,2048]{1,0:T(8,128)(2,1)S(1)}, bf16[128,2048]{1,0:T(8,128)(2,1)S(1)}, u32[]{:S(2)}, u32[]{:S(2)}) collective-permute-start(bf16[128,2048]{1,0:T(8,128)(2,1)S(1)} %maximum_select_fusion.1), channel_id=1, source_target_pairs={{0,8},{1,9},{2,10},{3,11},{4,12},{5,13},{6,14},{7,15},{8,0},{9,1},... | collective-permute-start | bytes 1572872 | tf_op jit(solution)/shard_map/ppermute | solution.py:27
  52.2 17.0 %all-to-all-start = ((bf16[2,128,2048]{2,1,0:T(8,128)(2,1)}), bf16[2,128,2048]{2,1,0:T(8,128)(2,1)S(1)}, u32[]{:S(2)}, u32[]{:S(2)}) async-start(bf16[2,128,2048]{2,1,0:T(8,128)(2,1)} %bitcast.1), calls=%async_computation.1 | async-start | bytes 2097152 | tf_op jit(solution)/shard_map/all_to_all | solution.py:33
  55.8 77.5 %all-gather.9.cloned.1.call-start = ((), (), s32[]{:S(2)}) async-start(), calls=%async_computation.5 | async-start | bytes 1114112 | tf_op jit(solution)/shard_map/all_gather | solution.py:37
  73.0 153.4 %all-gather.11.cloned.1.call-start = ((), (), s32[]{:S(2)}) async-start(), calls=%async_computation.6 | async-start | bytes 11010048 | tf_op jit(solution)/shard_map/all_gather | solution.py:38
  73.6 32.4 %copy-start.2 = (u32[32]{0:T(128)S(1)}, u32[32]{0:T(128)}, u32[]{:S(2)}) copy-start(u32[32]{0:T(128)} %constant.35) | copy-start | bytes 388
  73.6 173.8 %reduce-scatter.2.cloned.1.call-start = ((), (), s32[]{:S(2)}) async-start(), calls=%async_computation.3 | async-start | bytes 1376256 | tf_op jit(solution)/shard_map/reduce_scatter | solution.py:22
  106.6 188.2 %copy-start.1 = (s32[2]{0:T(128)S(1)}, s32[2]{0:T(128)}, u32[]{:S(2)}) copy-start(s32[2]{0:T(128)} %param.13) | copy-start | bytes 28
  287.8 7.6 %copy-start.3 = (f32[128]{0:T(128)}, f32[128]{0:T(128)S(1)}, u32[]{:S(2)}) copy-start(f32[128]{0:T(128)S(1)} %psum.7) | copy-start | bytes 1540
Sparse Core Ops, SparseCore 0:
  9.6 35.8 all-gather.6
  47.7 47.4 all-gather.4
  97.4 35.8 all-gather.8
  134.7 91.6 all-gather.10
  228.5 18.8 reduce-scatter.1
